TPU v7x, 128 devices: a whole 4x4x4 slice. The times are simulated.
128 devices in a mesh: tm: 64 (over x, z, y_lo, core), row: 2 (over y_hi).
Axes of the slice: x: 4, y: 4 (y_hi: 2, y_lo: 2; y = y_hi * 2 + y_lo), z: 4, core: 2. Of those that a mesh axis runs over, the one named last changes fastest.
Arguments:
- slice_ops: bfloat16 [64, 2048, 2048], P('tm', 'row'), may hold values from -6 to 6
- base_op: bfloat16 [2048, 2048], replicated, may hold values from -6 to 6
- load_table: float32 [16, 2048], replicated, may hold values from -1 to 1
- phase_idx: int32 [64, 2], P('tm'), may hold values from 0 to 15
- step_counts: int32 [64, 2], P('tm'), may hold values from 1 to 8
Outputs:
- windows: bfloat16 [64, 2048, 2048], P('tm', 'row')
All inputs are finite; a program needn't handle non-finite values.
Results may differ from a plain program's by a relative error of at most 0.012.
Values may be sent and summed in bfloat16 or wider, within the bound.
No kernel may reach another device: no remote copies, remote signals or barrier semaphores. Data moves between devices by JAX's collectives and lax.ppermute only.
A program may use at most 128 MiB of HBM per device.

v0:
```python
import math
import jax
import jax.numpy as jnp
from jax import lax
from jax.sharding import PartitionSpec as P

LEVELS = 2


def shifted(value, axis, steps):
    count = lax.axis_size(axis)
    pairs = [(source, (source + steps) % count) for source in range(count)]
    return lax.ppermute(value, axis, pairs)


def shards(slice_ops, base_op, load_table, phase_idx, step_counts):
    state_size = base_op.shape[0]
    norm_scale = 1.0 / math.sqrt(state_size)
    phase_count = load_table.shape[0]
    index_row = phase_idx[0]
    count_row = step_counts[0].astype(jnp.float32)
    one_hot = (
        index_row[:, None] == lax.broadcasted_iota(jnp.int32, (index_row.shape[0], phase_count), 1)
    ).astype(jnp.float32)
    table_rows = jnp.dot(one_hot, load_table, precision=lax.Precision.HIGHEST)
    gain_rows = jnp.exp(0.1 * count_row[:, None] * table_rows)
    right_factor = (base_op * gain_rows[0]).astype(jnp.bfloat16)
    left_factor = (slice_ops[0] * gain_rows[1]).astype(jnp.bfloat16)
    product = jnp.dot(left_factor, right_factor, preferred_element_type=jnp.float32)
    current = (product * norm_scale).astype(jnp.bfloat16)
    for depth_level in range(LEVELS):
        distance = 2**depth_level
        whole = lax.all_gather(current, "row", axis=0, tiled=True)
        earlier = shifted(whole, "tm", distance)
        combined = jnp.dot(current, earlier, preferred_element_type=jnp.float32)
        current = (combined * norm_scale).astype(jnp.bfloat16)
    return current[None]


def solution(mesh):
    return jax.shard_map(
        shards,
        mesh=mesh,
        in_specs=(P("tm", "row", None), P(), P(), P("tm", None), P("tm", None)),
        out_specs=P("tm", "row", None),
        check_vma=False,
    )
```

profile of v0, /device:TPU:0, one launch (start us, length us, event | category | flops | bytes accessed | tf_op | source)
XLA Modules:
  0.0 551.6 jit_solution(3729319134731721616)
XLA Ops:
  6.5 0.0 copy-start
  6.5 0.0 all-gather.3.cloned.1.call-start
  6.5 0.7 multiply_bitcast_fusion
  7.2 0.2 copy-done
  7.5 0.9 fusion.7
  8.4 13.8 %multiply_convert_fusion.4 = bf16[1024,2048]{1,0:T(8,128)(2,1)} fusion(bf16[2048,2048]{1,0:T(8,128)(2,1)} %param.6, f32[2048]{0:T(1024)S(1)} %bitcast.19, bf16[1,1024,2048]{2,1,0:T(8,128)(2,1)} %param.5, f32[2048]{0:T(1024)S(1)} %bitcast.18), kind=kOutput, calls=%fused_computation.6 | convolution fusion | flops 8613003264 | bytes 16793600 | tf_op jit(solution)/shard_map/dot_general | solution.py:29
  22.2 0.0 all-gather.3.cloned.1.call-update
  22.2 0.0 all-gather.5.cloned.1.call-start
  22.3 110.6 %all-gather.3.cloned.1.call-done = bf16[2048,2048]{1,0:T(8,128)(2,1)} async-done(((bf16[1024,2048]{1,0:T(8,128)(2,1)}), bf16[2048,2048]{1,0:T(8,128)(2,1)}) %all-gather.3.cloned.1.call-update) | async-done | bytes 8388624 | tf_op jit(solution)/shard_map/all_gather | solution.py:33
  132.9 0.0 collective-permute-start
  132.9 97.3 %collective-permute-done = bf16[2048,2048]{1,0:T(8,128)(2,1)S(1)} collective-permute-done((bf16[2048,2048]{1,0:T(8,128)(2,1)}, bf16[2048,2048]{1,0:T(8,128)(2,1)S(1)}, u32[]{:S(2)}, u32[]{:S(2)}) %collective-permute-start) | collective-permute-done | bytes 8388640 | tf_op jit(solution)/shard_map/ppermute | solution.py:13
  230.2 12.1 %multiply_convert_fusion.3 = bf16[1024,2048]{1,0:T(8,128)(2,1)} fusion(bf16[1024,2048]{1,0:T(8,128)(2,1)} %multiply_convert_fusion.4, bf16[2048,2048]{1,0:T(8,128)(2,1)S(1)} %collective-permute-done), kind=kOutput, calls=%fused_computation.5 | convolution fusion | flops 8594128896 | bytes 16777216 | tf_op jit(solution)/shard_map/dot_general | solution.py:35
  242.3 0.0 all-gather.5.cloned.1.call-update
  242.4 103.7 %all-gather.5.cloned.1.call-done = bf16[2048,2048]{1,0:T(8,128)(2,1)} async-done(((bf16[1024,2048]{1,0:T(8,128)(2,1)}), bf16[2048,2048]{1,0:T(8,128)(2,1)}) %all-gather.5.cloned.1.call-update) | async-done | bytes 8388624 | tf_op jit(solution)/shard_map/all_gather | solution.py:33
  346.1 0.6 collective-permute-start.1
  346.7 186.0 %collective-permute-done.1 = bf16[2048,2048]{1,0:T(8,128)(2,1)S(1)} collective-permute-done((bf16[2048,2048]{1,0:T(8,128)(2,1)}, bf16[2048,2048]{1,0:T(8,128)(2,1)S(1)}, u32[]{:S(2)}, u32[]{:S(2)}) %collective-permute-start.1) | collective-permute-done | bytes 8388640 | tf_op jit(solution)/shard_map/ppermute | solution.py:13
  532.7 12.1 %fusion.6 = bf16[1,1024,2048]{2,1,0:T(8,128)(2,1)} fusion(bf16[1024,2048]{1,0:T(8,128)(2,1)} %multiply_convert_fusion.3, bf16[2048,2048]{1,0:T(8,128)(2,1)S(1)} %collective-permute-done.1), kind=kOutput, calls=%fused_computation.10 | convolution fusion | flops 8594128896 | bytes 16777216 | tf_op jit(solution)/shard_map/dot_general | solution.py:35
  (1 shorter events, 0.0 us)
Async XLA Ops:
  6.5 0.9 copy-start
  6.5 126.4 %all-gather.3.cloned.1.call-start = ((), (), s32[]{:S(2)}) async-start(), calls=%async_computation | async-start | bytes 12582912 | tf_op jit(solution)/shard_map/all_gather | solution.py:33
  22.2 323.8 %all-gather.5.cloned.1.call-start = ((), (), s32[]{:S(2)}) async-start(), calls=%async_computation.1 | async-start | bytes 12582912 | tf_op jit(solution)/shard_map/all_gather | solution.py:33
  132.9 97.3 %collective-permute-start = (bf16[2048,2048]{1,0:T(8,128)(2,1)}, bf16[2048,2048]{1,0:T(8,128)(2,1)S(1)}, u32[]{:S(2)}, u32[]{:S(2)}) collective-permute-start(bf16[2048,2048]{1,0:T(8,128)(2,1)} %all-gather.3.cloned.1.call-done), channel_id=1, source_target_pairs={{0,2},{2,4},{4,6},{6,8},{8,10},{10,12},{12,14},{14,16},{16,18},{18... | collective-permute-start | bytes 25165832 | tf_op jit(solution)/shard_map/ppermute | solution.py:13
  346.1 186.6 %collective-permute-start.1 = (bf16[2048,2048]{1,0:T(8,128)(2,1)}, bf16[2048,2048]{1,0:T(8,128)(2,1)S(1)}, u32[]{:S(2)}, u32[]{:S(2)}) collective-permute-start(bf16[2048,2048]{1,0:T(8,128)(2,1)} %all-gather.5.cloned.1.call-done), channel_id=1, source_target_pairs={{0,4},{2,6},{4,8},{6,10},{8,12},{10,14},{12,16},{14,18},{16,20},{1... | collective-permute-start | bytes 25165832 | tf_op jit(solution)/shard_map/ppermute | solution.py:13
Sparse Core Ops, SparseCore 0:
  22.3 110.5 all-gather.2
  242.5 103.5 all-gather.4
where the time goes:
time: 552 us
  waiting for transfers between devices  498 us (90%)
  matrix products  38.9 us (7%)
  between operations  13.4 us (2%)
    ppermute x2, waiting for transfers between devices, shifted(): return lax.ppermute(value, axis, pairs)  283 us
    all_gather x2, waiting for transfers between devices, shards(): whole = lax.all_gather(current, 'row', axis=0, tiled=True)  214 us
    dot_general x2, matrix products, shards(): combined = jnp.dot(current, earlier, preferred_element_type=jnp.float32)  24.2 us
    dot_general x1, matrix products, shards(): jnp.dot(left_factor, right_factor, preferred_element_type=jnp.float32)  13.8 us
  transfers between devices with their start and end apart: 4, of which 4 were waited for; matrix products, arithmetic and copies ran while one was open for 0% of the time, Pallas kernels for 0%

commit v1 on v0

--- a/solution.py
+++ b/solution.py
@@ -30,7 +30,10 @@
     current = (product * norm_scale).astype(jnp.bfloat16)
     for depth_level in range(LEVELS):
         distance = 2**depth_level
-        whole = lax.all_gather(current, "row", axis=0, tiled=True)
+        peers = lax.axis_size("row")
+        blocks = jnp.stack([current for _ in range(peers)])
+        blocks = lax.all_to_all(blocks, "row", split_axis=0, concat_axis=0)
+        whole = jnp.concatenate(blocks, axis=0)
         earlier = shifted(whole, "tm", distance)
         combined = jnp.dot(current, earlier, preferred_element_type=jnp.float32)
         current = (combined * norm_scale).astype(jnp.bfloat16)

time: 552 us -> 523 us (0.947)
  waiting for transfers between devices: 498 us -> 281 us
  blocking collectives: 0 us -> 193 us
  between operations: 13.4 us -> 0.03 us
  other arithmetic: 0.69 us -> 12.1 us
    all_gather x2 -> x0, waiting for transfers between devices: 214 us -> none  [shards(): whole = lax.all_gather(current, 'row', axis=0, tiled=True)]
    all_to_all x0 -> x2, blocking collectives: none -> 193 us  [shards(): blocks = lax.all_to_all(blocks, 'row', split_axis=0, concat_axis=0)]
    another operation x0 -> x2, other arithmetic: none -> 11.4 us  [shards(): blocks = jnp.stack([current for _ in range(peers)])]
  transfers between devices with their start and end apart: 4 -> 2, of which waited for: 4 -> 2; matrix products, arithmetic and copies ran while one was open for 0% -> 0% of each run, Pallas kernels for 0% -> 0%
where the time goes in v1:
time: 523 us; the launch traced here: 522 us
  waiting for transfers between devices  281 us (54%)
  blocking collectives  193 us (37%)
  matrix products  34.1 us (7%)
  other arithmetic  12.1 us (2%)
    ppermute x2, waiting for transfers between devices, shifted(): return lax.ppermute(value, axis, pairs)  281 us
    all_to_all x2, blocking collectives, shards(): blocks = lax.all_to_all(blocks, 'row', split_axis=0, concat_axis=0)  193 us
    dot_general x2, matrix products, shards(): combined = jnp.dot(current, earlier, preferred_element_type=jnp.float32)  20.7 us
    dot_general x1, matrix products, shards(): jnp.dot(left_factor, right_factor, preferred_element_type=jnp.float32)  12.5 us
    another operation x2, other arithmetic, shards(): blocks = jnp.stack([current for _ in range(peers)])  11.4 us
  transfers between devices with their start and end apart: 2, of which 2 were waited for; matrix products, arithmetic and copies ran while one was open for 0% of the time, Pallas kernels for 0%

profile of v1, /device:TPU:0, one launch (start us, length us, event | category | flops | bytes accessed | tf_op | source)
XLA Modules:
  0.0 522.5 jit_solution(493263166934882879)
XLA Ops:
  0.0 0.0 copy-start
  0.0 0.7 multiply_bitcast_fusion
  0.7 0.2 copy-done
  0.9 0.9 fusion.7
  1.8 12.5 %multiply_convert_fusion.4 = bf16[1024,2048]{1,0:T(8,128)(2,1)S(1)} fusion(bf16[2048,2048]{1,0:T(8,128)(2,1)} %param.6, f32[2048]{0:T(1024)S(1)} %bitcast.27, bf16[1,1024,2048]{2,1,0:T(8,128)(2,1)} %param.5, f32[2048]{0:T(1024)S(1)} %bitcast.26), kind=kOutput, calls=%fused_computation.8 | convolution fusion | flops 8613003264 | bytes 16793600 | tf_op jit(solution)/shard_map/dot_general | solution.py:29
  14.4 4.0 pad_maximum_fusion
  18.3 98.8 %all_to_all.10 = bf16[2,1024,2048]{2,1,0:T(8,128)(2,1)S(1)} all-to-all(bf16[2,1024,2048]{2,1,0:T(8,128)(2,1)} %pad_maximum_fusion), channel_id=1, replica_groups=mesh['tm'=64,'row'=2] {'row'}, dimensions={0} | all-to-all | bytes 16777216 | tf_op jit(solution)/shard_map/all_to_all | solution.py:35
  117.1 0.0 collective-permute-start
  117.1 97.1 %collective-permute-done = bf16[2048,2048]{1,0:T(8,128)(2,1)S(1)} collective-permute-done((bf16[2048,2048]{1,0:T(8,128)(2,1)S(1)}, bf16[2048,2048]{1,0:T(8,128)(2,1)S(1)}, u32[]{:S(2)}, u32[]{:S(2)}) %collective-permute-start) | collective-permute-done | bytes 8388640 | tf_op jit(solution)/shard_map/ppermute | solution.py:13
  214.2 10.4 %multiply_convert_fusion.3 = bf16[1024,2048]{1,0:T(8,128)(2,1)} fusion(bf16[1024,2048]{1,0:T(8,128)(2,1)S(1)} %multiply_convert_fusion.4, bf16[2048,2048]{1,0:T(8,128)(2,1)S(1)} %collective-permute-done), kind=kOutput, calls=%fused_computation.7 | convolution fusion | flops 8594128896 | bytes 16777216 | tf_op jit(solution)/shard_map/dot_general | solution.py:38
  224.5 7.5 %pad_maximum_fusion.1 = bf16[2,1024,2048]{2,1,0:T(8,128)(2,1)} fusion(bf16[1,1024,2048]{2,1,0:T(8,128)(2,1)} %bitcast.25), kind=kLoop, calls=%fused_computation.3 | loop fusion | flops 4194304 | bytes 12582912 | tf_op jit(solution)/shard_map/stack | solution.py:34
  232.0 0.0 copy-start.2
  232.0 94.2 %all_to_all.11 = bf16[2,1024,2048]{2,1,0:T(8,128)(2,1)S(1)} all-to-all(bf16[2,1024,2048]{2,1,0:T(8,128)(2,1)} %pad_maximum_fusion.1), channel_id=1, replica_groups=mesh['tm'=64,'row'=2] {'row'}, dimensions={0} | all-to-all | bytes 16777216 | tf_op jit(solution)/shard_map/all_to_all | solution.py:35
  326.2 1.8 collective-permute-start.1
  328.0 184.1 %collective-permute-done.1 = bf16[2048,2048]{1,0:T(8,128)(2,1)S(1)} collective-permute-done((bf16[2048,2048]{1,0:T(8,128)(2,1)S(1)}, bf16[2048,2048]{1,0:T(8,128)(2,1)S(1)}, u32[]{:S(2)}, u32[]{:S(2)}) %collective-permute-start.1) | collective-permute-done | bytes 8388640 | tf_op jit(solution)/shard_map/ppermute | solution.py:13
  512.1 0.0 copy-done.2
  512.1 0.0 copy-start.1
  512.1 10.4 %fusion.6 = bf16[1,1024,2048]{2,1,0:T(8,128)(2,1)} fusion(bf16[1024,2048]{1,0:T(8,128)(2,1)S(1)} %copy-done.2, bf16[2048,2048]{1,0:T(8,128)(2,1)S(1)} %collective-permute-done.1), kind=kOutput, calls=%fused_computation.12 | convolution fusion | flops 8594128896 | bytes 16777216 | tf_op jit(solution)/shard_map/dot_general | solution.py:38
  522.5 0.0 copy-done.1
  (1 shorter events, 0.0 us)
Async XLA Ops:
  0.0 0.9 copy-start
  117.1 97.1 %collective-permute-start = (bf16[2048,2048]{1,0:T(8,128)(2,1)S(1)}, bf16[2048,2048]{1,0:T(8,128)(2,1)S(1)}, u32[]{:S(2)}, u32[]{:S(2)}) collective-permute-start(bf16[2048,2048]{1,0:T(8,128)(2,1)S(1)} %bitcast.22), channel_id=1, source_target_pairs={{0,2},{2,4},{4,6},{6,8},{8,10},{10,12},{12,14},{14,16},{16,18},{18... | collective-permute-start | bytes 25165832 | tf_op jit(solution)/shard_map/ppermute | solution.py:13
  232.0 280.1 %copy-start.2 = (bf16[1024,2048]{1,0:T(8,128)(2,1)S(1)}, bf16[1024,2048]{1,0:T(8,128)(2,1)}, u32[]{:S(2)}) copy-start(bf16[1024,2048]{1,0:T(8,128)(2,1)} %multiply_convert_fusion.3) | copy-start | bytes 12582916
  326.2 185.9 %collective-permute-start.1 = (bf16[2048,2048]{1,0:T(8,128)(2,1)S(1)}, bf16[2048,2048]{1,0:T(8,128)(2,1)S(1)}, u32[]{:S(2)}, u32[]{:S(2)}) collective-permute-start(bf16[2048,2048]{1,0:T(8,128)(2,1)S(1)} %bitcast.23), channel_id=1, source_target_pairs={{0,4},{2,6},{4,8},{6,10},{8,12},{10,14},{12,16},{14,18},{16,20},{1... | collective-permute-start | bytes 25165832 | tf_op jit(solution)/shard_map/ppermute | solution.py:13
  512.1 10.4 %copy-start.1 = (f32[16,2048]{1,0:T(8,128)S(1)}, f32[16,2048]{1,0:T(8,128)}, u32[]{:S(2)}) copy-start(f32[16,2048]{1,0:T(8,128)} %param.7) | copy-start | bytes 393220
